TPU v7x, 32 devices: a whole 2x2x4 slice. The times are simulated.
32 devices in a mesh: groups: 2 (over y), seq: 4 (over z), chan: 2 (over x), rep: 2 (over core).
Axes of the slice: x: 2, y: 2, z: 4, core: 2. Of those that a mesh axis runs over, the one named last changes fastest.
Arguments:
- query_proj: bfloat16 [2048, 8192], P(('groups', 'seq'), ('chan', 'rep')), parts along dimension 0, may hold values from -6 to 6
- key_proj: bfloat16 [2048, 8192], P(('groups', 'seq'), ('chan', 'rep')), parts along dimension 0, may hold values from -6 to 6
- value_proj: bfloat16 [2048, 8192], P(('groups', 'seq'), ('chan', 'rep')), parts along dimension 0, may hold values from -6 to 6
- short_taps: bfloat16 [7, 8192], P(None, ('chan', 'rep')), may hold values from -2 to 2
- medium_taps: bfloat16 [128, 512], P(None, ('chan', 'rep')), may hold values from -0.5 to 0.5
- modal_poles: float32 [4, 512, 16], P(None, ('chan', 'rep')), may hold values from -3.1416 to 3.1416, as said below
- skip_gain: float32 [8192], P(('chan', 'rep')), may hold values from 0.5 to 1.5
- norm_gain: float32 [8192], P(('chan', 'rep')), may hold values from 0.5 to 1.5
- unembed: bfloat16 [8192, 512], P(('chan', 'rep')), may hold values from -0.1875 to 0.1875
- token_ids: int32 [2048], P(('groups', 'seq')), parts along dimension 0, may hold values from 0 to 511
- genome_lengths: int32 [16], P('groups'), parts along dimension 0, may hold values from 1 to 512, 1024 in all
Outputs:
- token_logprob: float32 [2048], P(('groups', 'seq')), parts along dimension 0
- genome_score: float32 [16], P('groups'), parts along dimension 0
There are 2 independent parts, one for each index of `groups`. A program takes and returns all parts, laid end to end along the dimension named above; an argument that names none is the same for every part. Nothing has to cross between parts.
Inputs may be any that keep to these rules, and one draw needn't show every extreme that they name: `genome_lengths`: the 8 genomes are packed end to end from position 0; their lengths sum to 1024. `modal_poles`: row 0 holds positive decay rates, row 1 angles, rows 2 and 3 residues.
All inputs are finite; a program needn't handle non-finite values.
Results may differ from a plain program's by a relative error of at most 0.0033.
Values may be sent and summed in bfloat16 or wider, within the bound.
No kernel may reach another device: no remote copies, remote signals or barrier semaphores. Data moves between devices by JAX's collectives and lax.ppermute only.
A program may use at most 128 MiB of HBM per device.

v0:
```python
import jax
import jax.numpy as jnp
from jax import lax
from jax.sharding import PartitionSpec as P

D = 8192
GROUP = 16
tile_rows = 128
short_margin = 8
norm_eps = 1e-05


def from_behind(shard, axis, by):
    count = lax.axis_size(axis)
    pairs = [(i, i + by) for i in range(count) if 0 <= i + by < count]
    return lax.ppermute(shard, axis, pairs)


def entering_2(part, axis, combine, identity):
    place = lax.axis_index(axis)
    gathered = jax.tree.map(lambda a: lax.all_gather(a, axis), part)
    state = jax.tree.map(lambda a, e: jnp.zeros_like(a) + jnp.asarray(e, a.dtype), part, identity)

    def one(step, state):
        return combine(
            state, jax.tree.map(lambda a: lax.dynamic_index_in_dim(a, step, 0, False), gathered)
        )

    return lax.fori_loop(0, place, one, state)


def segment_ids(positions, genome_lengths):
    starts = jnp.cumsum(genome_lengths) - genome_lengths
    at_or_past = (positions[:, None] >= starts[None, :]).astype(jnp.int32)
    return jnp.sum(at_or_past, axis=1) - 1


def short_filter(keys_in, values_in, seg_list, out_rows, short_taps):
    gated = keys_in.astype(jnp.float32) * values_in.astype(jnp.float32)
    total_rows = keys_in.shape[0]
    lead_rows = total_rows - out_rows
    own_segs = seg_list[lead_rows:]
    result = jnp.zeros((out_rows, keys_in.shape[1]), jnp.float32)
    for lag_index in range(short_taps.shape[0]):
        shifted = gated[lead_rows - lag_index : total_rows - lag_index]
        same_genome = (seg_list[lead_rows - lag_index : total_rows - lag_index] == own_segs).astype(
            jnp.float32
        )
        result = (
            result
            + short_taps[lag_index].astype(jnp.float32)[None, :] * shifted * same_genome[:, None]
        )
    return result.astype(jnp.bfloat16)


def medium_toeplitz(medium_taps):
    out_pos = jnp.arange(tile_rows, dtype=jnp.int32)[:, None]
    in_pos = jnp.arange(2 * tile_rows, dtype=jnp.int32)[None, :]
    lag_grid = out_pos + tile_rows - in_pos
    tap_count = medium_taps.shape[0]
    valid = (lag_grid >= 0) & (lag_grid < tap_count)
    gathered = jnp.take(medium_taps, jnp.clip(lag_grid, 0, tap_count - 1), axis=0)
    masked = jnp.where(valid[:, :, None], gathered, jnp.zeros_like(gathered))
    return jnp.transpose(masked, (2, 0, 1))


def modal_tables(modal_poles):
    decay_rate = modal_poles[0]
    angles = modal_poles[1]
    residue_re = modal_poles[2]
    residue_im = modal_poles[3]
    powers = jnp.arange(tile_rows + 1).astype(jnp.float32)[:, None, None]
    magnitude = jnp.exp(-powers * decay_rate[None])
    power_re = magnitude * jnp.cos(powers * angles[None])
    power_im = magnitude * jnp.sin(powers * angles[None])
    kernel_re = residue_re[None] * power_re - residue_im[None] * power_im
    kernel_im = residue_re[None] * power_im + residue_im[None] * power_re
    kernel = jnp.sum(kernel_re[:tile_rows], axis=2)
    lag_grid = (
        jnp.arange(tile_rows, dtype=jnp.int32)[:, None]
        - jnp.arange(tile_rows, dtype=jnp.int32)[None, :]
    )
    taken = jnp.take(kernel, jnp.clip(lag_grid, 0, tile_rows - 1), axis=0)
    toeplitz = jnp.transpose(
        jnp.where((lag_grid >= 0)[:, :, None], taken, jnp.zeros_like(taken)), (2, 0, 1)
    )
    outward = jnp.transpose(jnp.concatenate((kernel_re[1:], -kernel_im[1:]), axis=2), (1, 0, 2))
    inward = jnp.transpose(
        jnp.concatenate((power_re[tile_rows - 1 :: -1], power_im[tile_rows - 1 :: -1]), axis=2),
        (1, 0, 2),
    )
    return (toeplitz, outward, inward, power_re[tile_rows], power_im[tile_rows])


def split_table(table):
    upper = table.astype(jnp.bfloat16)
    lower = (table - upper.astype(jnp.float32)).astype(jnp.bfloat16)
    return (upper, lower)


def complex_link(earlier, later):
    early_are, early_aim, early_sre, early_sim = earlier
    late_are, late_aim, late_sre, late_sim = later
    lead_re = late_are[..., None, :]
    lead_im = late_aim[..., None, :]
    return (
        late_are * early_are - late_aim * early_aim,
        late_are * early_aim + late_aim * early_are,
        lead_re * early_sre - lead_im * early_sim + late_sre,
        lead_re * early_sim + lead_im * early_sre + late_sim,
    )


def log_probs(logits, targets):
    vocab_ids = jnp.arange(logits.shape[1], dtype=jnp.int32)
    picked = jnp.sum(
        jnp.where(targets[:, None] == vocab_ids[None, :], logits, jnp.zeros_like(logits)), axis=1
    )
    return picked - jnp.log(jnp.sum(jnp.exp(logits), axis=1))


def channel_logits(normed_cols, unembed):
    return lax.dot_general(
        normed_cols, unembed, (((0,), (0,)), ((), ())), preferred_element_type=jnp.float32
    )


def per_device(
    query_proj,
    key_proj,
    value_proj,
    short_taps,
    medium_taps,
    modal_poles,
    skip_gain,
    norm_gain,
    unembed,
    token_ids,
    genome_lengths,
):
    highest = lax.Precision.HIGHEST
    row_count, chan_count = query_proj.shape
    group_count = chan_count // GROUP
    mode_count = modal_poles.shape[2]
    tile_count = row_count // tile_rows
    first_row = lax.axis_index("seq") * row_count
    segments = segment_ids(first_row + jnp.arange(row_count, dtype=jnp.int32), genome_lengths)
    edge_pair = from_behind(
        jnp.stack((key_proj[row_count - short_margin :], value_proj[row_count - short_margin :])),
        "seq",
        1,
    )
    ext_segs = segment_ids(
        first_row - short_margin + jnp.arange(row_count + short_margin, dtype=jnp.int32),
        genome_lengths,
    )
    filtered = short_filter(
        jnp.concatenate((edge_pair[0], key_proj)),
        jnp.concatenate((edge_pair[1], value_proj)),
        ext_segs,
        row_count,
        short_taps,
    )
    previous = from_behind(filtered[row_count - tile_rows :], "seq", 1)
    ext_short = jnp.concatenate((previous, filtered)).T.reshape(
        group_count, GROUP, row_count + tile_rows
    )
    medium_segs = segment_ids(
        first_row - tile_rows + jnp.arange(row_count + tile_rows, dtype=jnp.int32), genome_lengths
    )
    toeplitz = medium_toeplitz(medium_taps)

    def medium_block(tile_index):
        start = tile_index * tile_rows
        window = lax.dynamic_slice_in_dim(ext_short, start, 2 * tile_rows, 2)
        window_segs = lax.dynamic_slice_in_dim(medium_segs, start, 2 * tile_rows, 0)
        own_segs = lax.dynamic_slice_in_dim(segments, start, tile_rows, 0)
        same_genome = own_segs[:, None] == window_segs[None, :]
        matrix = jnp.where(same_genome[None], toeplitz, jnp.zeros_like(toeplitz))
        return jnp.einsum(
            "gts,gis->git", matrix, window, preferred_element_type=jnp.float32
        ).astype(jnp.bfloat16)

    signal = lax.map(medium_block, jnp.arange(tile_count, dtype=jnp.int32))
    long_toeplitz, outward, inward, decay_re, decay_im = modal_tables(modal_poles)
    toeplitz_upper, toeplitz_lower = split_table(long_toeplitz)
    inward_upper, inward_lower = split_table(inward)
    tile_segs = segments.reshape(tile_count, tile_rows)
    before = segment_ids(
        first_row + jnp.arange(tile_count, dtype=jnp.int32) * tile_rows - 1, genome_lengths
    )

    def intra_block(inputs):
        block_in, own_segs = inputs
        same_genome = (own_segs[:, None] == own_segs[None, :])[None]
        upper = jnp.where(same_genome, toeplitz_upper, jnp.zeros_like(toeplitz_upper))
        lower = jnp.where(same_genome, toeplitz_lower, jnp.zeros_like(toeplitz_lower))
        return jnp.einsum(
            "gts,gis->git", upper, block_in, preferred_element_type=jnp.float32
        ) + jnp.einsum("gts,gis->git", lower, block_in, preferred_element_type=jnp.float32)

    local_part = lax.map(intra_block, (signal, tile_segs))
    end_keep = (tile_segs == tile_segs[:, -1:])[:, None, None, :]
    masked_signal = jnp.where(end_keep, signal, jnp.zeros_like(signal))
    states = jnp.einsum(
        "gsm,jgis->jgim", inward_upper, masked_signal, preferred_element_type=jnp.float32
    ) + jnp.einsum(
        "gsm,jgis->jgim", inward_lower, masked_signal, preferred_element_type=jnp.float32
    )
    carried = (tile_segs[:, -1] == before).astype(jnp.float32)

    def chain_link(carry_in, inputs):
        block_states, kept_flag = inputs
        step = (
            decay_re * kept_flag,
            decay_im * kept_flag,
            block_states[..., :mode_count],
            block_states[..., mode_count:],
        )
        return (complex_link(carry_in, step), carry_in)

    state_zero = jnp.zeros((group_count, GROUP, mode_count), jnp.float32)
    start_carry = (
        jnp.ones((group_count, mode_count), jnp.float32),
        jnp.zeros((group_count, mode_count), jnp.float32),
        state_zero,
        state_zero,
    )
    summary, entering = lax.scan(chain_link, start_carry, (states, carried))
    incoming = entering_2(
        (summary[0], summary[1], summary[2], summary[3]),
        "seq",
        complex_link,
        (start_carry[0], start_carry[1], start_carry[2], start_carry[3]),
    )
    incoming_re = incoming[2]
    incoming_im = incoming[3]
    reach_re = entering[0][:, :, None, :]
    reach_im = entering[1][:, :, None, :]
    full_re = entering[2] + reach_re * incoming_re - reach_im * incoming_im
    full_im = entering[3] + reach_re * incoming_im + reach_im * incoming_re
    keep_mask = (tile_segs == before[:, None]).astype(jnp.float32)
    carried_part = (
        jnp.einsum(
            "gtm,jgim->jgit",
            outward,
            jnp.concatenate((full_re, full_im), axis=3),
            precision=highest,
        )
        * keep_mask[:, None, None, :]
    )
    longconv = (
        local_part
        + carried_part
        + skip_gain.reshape(group_count, GROUP)[None, :, :, None] * signal.astype(jnp.float32)
    )
    long_cols = jnp.transpose(longconv, (1, 2, 0, 3)).reshape(chan_count, row_count)
    mixed = (query_proj.T.astype(jnp.float32) * long_cols).astype(jnp.bfloat16)
    mixed_wide = mixed.astype(jnp.float32)
    squares = lax.psum(jnp.sum(mixed_wide * mixed_wide, axis=0), ("chan", "rep"))
    normed = (mixed_wide * lax.rsqrt(squares / D + norm_eps)[None, :] * norm_gain[:, None]).astype(
        jnp.bfloat16
    )
    partial_value = channel_logits(normed, unembed)
    logits = lax.psum(partial_value, ("chan", "rep"))
    logprob = log_probs(logits, token_ids)
    genome_index = jnp.arange(genome_lengths.shape[0], dtype=jnp.int32)
    genome_part = jnp.sum(
        jnp.where(
            segments[:, None] == genome_index[None, :],
            logprob[:, None],
            jnp.zeros((row_count, genome_lengths.shape[0]), jnp.float32),
        ),
        axis=0,
    )
    totals = lax.psum(genome_part, "seq")
    return (logprob, totals / genome_lengths.astype(jnp.float32))


def solution(mesh):
    return jax.shard_map(
        per_device,
        mesh=mesh,
        in_specs=(
            P(("groups", "seq"), ("chan", "rep")),
            P(("groups", "seq"), ("chan", "rep")),
            P(("groups", "seq"), ("chan", "rep")),
            P(None, ("chan", "rep")),
            P(None, ("chan", "rep")),
            P(None, ("chan", "rep"), None),
            P(("chan", "rep")),
            P(("chan", "rep")),
            P(("chan", "rep"), None),
            P(("groups", "seq")),
            P("groups"),
        ),
        out_specs=(P(("groups", "seq")), P("groups")),
        check_vma=False,
    )
```

profile of v0, /device:TPU:0, one launch (start us, length us, event | category | flops | bytes accessed | tf_op | source)
XLA Modules:
  0.0 474.0 jit_solution(14729307594950726324)
XLA Ops:
  7.2 0.9 slice_bitcast_fusion.2
  8.8 5.5 %collective-permute-start = (bf16[2,8,2048]{2,1,0:T(8,128)(2,1)}, bf16[2,8,2048]{2,1,0:T(8,128)(2,1)}, u32[]{:S(2)}, u32[]{:S(2)}) collective-permute-start(bf16[2,8,2048]{2,1,0:T(8,128)(2,1)} %pad_maximum_fusion.1), channel_id=1, source_target_pairs={{0,4},{4,8},{8,12},{1,5},{5,9},{9,13},{2,6},{6,10},{10,14},{3,7},{... | collective-permute-start | bytes 196616 | tf_op jit(solution)/shard_map/ppermute | solution.py:16
  14.8 0.8 reduce-window.9
  15.6 0.7 bitcast_subtract_fusion.1
  16.3 0.7 compare_convert_fusion.8
  17.0 1.7 slice_convert_fusion.6
  20.1 114.1 %gather_fusion = bf16[32768,128]{1,0:T(8,128)(2,1)} fusion(bf16[128,128]{1,0:T(8,128)(2,1)S(1)} %copy-done.1, s32[32768]{0:T(1024)S(1)} %broadcast_clamp_fusion), kind=kCustom, calls=%fused_computation | custom fusion | bytes 16908288 | tf_op jit(solution)/shard_map/jit(_take)/gather | solution.py:62
  134.3 12.9 %copy.87 = bf16[128,256,128]{1,0,2:T(8,128)(2,1)} copy(bf16[128,256,128]{2,1,0:T(8,128)(2,1)} %bitcast.210) | data formatting | bytes 16777216 | tf_op jit(solution)/shard_map/jit(_take)/gather | solution.py:62
  147.9 9.5 %fusion.47 = (f32[129,128,16]{0,2,1:T(8,128)}, f32[129,128,16]{0,2,1:T(8,128)S(1)}, f32[129,128,16]{0,2,1:T(8,128)}) fusion(f32[128,16]{1,0:T(8,128)S(1)} %copy.90, f32[129]{0:T(256)S(1)} %iota_convert_fusion, f32[128,16]{1,0:T(8,128)S(1)} %copy.89, f32[129]{0:T(256)S(1)} %fusion.95, f32[128,16]{1,0:T(8,128)S(1)} %copy.91, f32[128,16]{1,0:T(8,128)S(1)} %copy.88), kind=kLoop, calls=%fused_computation.66 | loop fusion | flops 1849344 | bytes 3204104 | tf_op jit(solution)/shard_map/mul | solution.py:75
  157.4 1.4 fusion.101
  158.9 54.5 %gather_fusion.1 = f32[16384,128]{1,0:T(8,128)} fusion(f32[128,128]{1,0:T(8,128)S(1)} %copy.92, s32[16384]{0:T(1024)S(1)} %fusion.89), kind=kCustom, calls=%fused_computation.1 | custom fusion | bytes 16842752 | tf_op jit(solution)/shard_map/jit(_take)/gather | solution.py:83
  213.4 9.3 %copy.93 = f32[128,128,128]{1,0,2:T(8,128)} copy(f32[128,128,128]{2,1,0:T(8,128)} %bitcast.211) | data formatting | bytes 16777216 | tf_op jit(solution)/shard_map/jit(_take)/gather | solution.py:83
  222.7 4.5 fusion.76
  227.9 7.5 %select_bitcast_fusion = bf16[128,128,256]{2,1,0:T(8,128)(2,1)} fusion(bf16[128,256,128]{1,0,2:T(8,128)(2,1)} %copy.87, pred[128,256]{1,0:T(8,128)(4,1)S(1)} %get-tuple-element.472, pred[128,256]{1,0:T(8,128)(4,1)S(1)} %get-tuple-element.471), kind=kLoop, calls=%fused_computation.56 | loop fusion | flops 8388608 | bytes 16842752 | tf_op jit(solution)/shard_map/jit(_where)/select_n | solution.py:63
  235.4 6.8 %fusion.42 = bf16[128,128,128]{2,1,0:T(8,128)(2,1)} fusion(f32[128,128,128]{1,0,2:T(8,128)} %copy.93, pred[128,128]{1,0:T(8,128)(4,1)S(1)} %get-tuple-element.476, pred[128,128]{1,0:T(8,128)(4,1)S(1)} %get-tuple-element.475), kind=kLoop, calls=%fused_computation.54 | loop fusion | flops 12582912 | bytes 12615680 | tf_op jit(solution)/shard_map/convert_element_type | solution.py:97
  242.7 2.4 slice.179
  245.1 1.1 slice.180
  246.2 2.3 rev.6
  248.5 2.3 rev.7
  250.8 1.6 copy.94
  252.4 1.6 copy.95
  254.1 0.8 mul.500
  254.9 2.3 copy.85
  257.2 0.8 slice_bitcast_fusion
  258.1 1.9 convert_multiply_fusion.2
  260.1 3.0 fusion.51
  263.2 3.1 collective-permute-start.1
  266.3 3.4 bitcast_convert_fusion
  269.7 7.3 %collective-permute-done.1 = bf16[128,2048]{1,0:T(8,128)(2,1)S(1)} collective-permute-done((bf16[128,2048]{1,0:T(8,128)(2,1)S(1)}, bf16[128,2048]{1,0:T(8,128)(2,1)S(1)}, u32[]{:S(2)}, u32[]{:S(2)}) %collective-permute-start.1) | collective-permute-done | bytes 524320 | tf_op jit(solution)/shard_map/ppermute | solution.py:16
  277.0 1.3 maximum_bitcast_fusion.5
  278.2 2.6 copy.86
  280.9 15.2 %while.64 = (s32[]{:T(128)}, bf16[2,128,16,128]{3,2,1,0:T(8,128)(2,1)S(1)}, s32[2]{0:T(128)S(1)}, bf16[128,16,384]{2,1,0:T(8,128)(2,1)}, s32[256]{0:T(256)S(1)},...) while((s32[]{:T(128)}, bf16[2,128,16,128]{3,2,1,0:T(8,128)(2,1)S(1)}, ...), condition=%wide.region_5.6_spmd.clone, body=%wide.region_4.5_spmd.sunk.clone | while | flops 138706944 | bytes 10032308 | solution.py:184
  282.4 6.1 %fusion.126 = bf16[2,128,16,128]{3,2,1,0:T(8,128)(2,1)S(1)} fusion(bf16[2,128,16,128]{3,2,1,0:T(8,128)(2,1)S(1)} %get-tuple-element.826, s32[]{:T(128)} %get-tuple-element.825, bf16[128,128,256]{2,1,0:T(8,128)(2,1)} %get-tuple-element.839, pred[128,256]{1,0:T(8,128)(4,1)S(1)} %broadcast_compare_fusion.7, ...), kind=kOutput, calls=%fused_computation.8.clone.1.clone | convolution fusion | flops 138674176 | bytes 9994756 | tf_op jit(solution)/shard_map/while/body/eval_jaxpr/gts,gis->git/dot_general | solution.py:180
  290.0 6.1 %fusion.126 = bf16[2,128,16,128]{3,2,1,0:T(8,128)(2,1)S(1)} fusion(bf16[2,128,16,128]{3,2,1,0:T(8,128)(2,1)S(1)} %get-tuple-element.826, s32[]{:T(128)} %get-tuple-element.825, bf16[128,128,256]{2,1,0:T(8,128)(2,1)} %get-tuple-element.839, pred[128,256]{1,0:T(8,128)(4,1)S(1)} %broadcast_compare_fusion.7, ...), kind=kOutput, calls=%fused_computation.8.clone.1.clone | convolution fusion | flops 138674176 | bytes 9994756 | tf_op jit(solution)/shard_map/while/body/eval_jaxpr/gts,gis->git/dot_general | solution.py:180
  296.1 2.4 fusion.69
  298.5 2.0 add_bitcast_fusion
  300.5 3.5 copy.98
  304.0 7.3 %while.67 = (s32[]{:T(128)}, f32[128,16]{0,1:T(8,128)S(1)}, f32[128,16]{0,1:T(8,128)S(1)}, f32[128,16,16]{0,2,1:T(8,128)S(1)}, f32[128,16,16]{0,2,1:T(8,128)S(1)...) while((s32[]{:T(128)}, f32[128,16]{0,1:T(8,128)S(1)}, ...), condition=%wide.region_11.12_spmd.clone.clone, body=%wide.region_10.11_spmd.clone.sunk.clone | while | flops 421891 | bytes 2000031 | solution.py:229
  305.3 0.7 bitcast_dynamic-update-slice_fusion.9
  306.0 1.0 dynamic-slice_bitcast_fusion.3
  308.9 0.7 bitcast_dynamic-update-slice_fusion.9
  309.6 1.0 dynamic-slice_bitcast_fusion.3
  311.3 17.7 %all-gather.2 = f32[512,16,16]{0,2,1:T(8,128)} all-gather(f32[128,16,16]{0,2,1:T(8,128)S(1)} %get-tuple-element.221), channel_id=4, replica_groups=mesh['groups'=2,'seq'=4,'chan'=2,'rep'=2] {'seq'}, dimensions={0}, use_global_device_ids=true | all-gather | bytes 655360 | tf_op jit(solution)/shard_map/all_gather | solution.py:21
  329.0 2.1 reshape.364
  331.1 15.5 %all-gather.3 = f32[512,16,16]{0,2,1:T(8,128)} all-gather(f32[128,16,16]{0,2,1:T(8,128)S(1)} %get-tuple-element.222), channel_id=5, replica_groups=mesh['groups'=2,'seq'=4,'chan'=2,'rep'=2] {'seq'}, dimensions={0}, use_global_device_ids=true | all-gather | bytes 655360 | tf_op jit(solution)/shard_map/all_gather | solution.py:21
  346.5 2.0 reshape.365
  348.6 13.1 %all-gather = f32[512,16]{0,1:T(8,128)S(1)} all-gather(f32[128,16]{0,1:T(8,128)S(1)} %get-tuple-element.219), channel_id=2, replica_groups=mesh['groups'=2,'seq'=4,'chan'=2,'rep'=2] {'seq'}, dimensions={0}, use_global_device_ids=true | all-gather | bytes 40960 | tf_op jit(solution)/shard_map/all_gather | solution.py:21
  361.7 13.1 %all-gather.1 = f32[512,16]{0,1:T(8,128)S(1)} all-gather(f32[128,16]{0,1:T(8,128)S(1)} %get-tuple-element.220), channel_id=3, replica_groups=mesh['groups'=2,'seq'=4,'chan'=2,'rep'=2] {'seq'}, dimensions={0}, use_global_device_ids=true | all-gather | bytes 40960 | tf_op jit(solution)/shard_map/all_gather | solution.py:21
  375.1 1.1 multiply_subtract_fusion.2
  376.2 0.9 pad_maximum_fusion
  377.2 3.9 copy.103
  381.0 16.2 %while.65 = (s32[]{:T(128)}, f32[2,128,16,128]{3,2,0,1:T(8,128)}, bf16[2,128,16,128]{3,2,1,0:T(8,128)(2,1)S(1)}, s32[2,128]{1,0:T(2,128)S(1)}, bf16[128,128,128]{2,1,0:T(8,128)(2,1)}, /*index=5*/bf16[128,128,128]{2,1,0:T(8,128)(2,1)}) while((s32[]{:T(128)}, f32[2,128,16,128]{3,2,0,1:T(8,128)}, ...), condition=%wide.region_8.9_spmd.clone, body=%wide.region_7.8_spmd.sunk.clone | while | flops 138690560 | bytes 29411944 | solution.py:202
  381.2 4.6 fusion.132
  385.8 3.4 fusion.133
  389.3 4.6 fusion.132
  393.9 3.4 fusion.133
  397.3 5.3 %fusion.66 = f32[128,16,2,128]{3,1,2,0:T(8,128)S(1)} fusion(f32[2,128,16,128]{3,2,0,1:T(8,128)} %get-tuple-element.216, f32[2,128,16,32]{3,2,0,1:T(8,128)} %copy.103, f32[128,128,16]{0,2,1:T(8,128)} %get-tuple-element.440, f32[128,128,16]{0,2,1:T(8,128)} %get-tuple-element.438, bf16[2,128,16,128]{3,2,1,0:T(8,128)(2,1)S(1)} %get-tuple-element.923, ...), kind=kOutput, calls=%fused_computation.96 | convolution fusion | flops 204472320 | bytes 7873536 | tf_op jit(solution)/shard_map/gtm,jgim->jgit/dot_general | solution.py:244
  402.6 1.1 copy.106
  403.7 1.3 copy-done.5
  405.4 5.7 %psum.21 = f32[256]{0:T(256)S(1)} all-reduce(f32[256]{0:T(256)S(1)} %fusion.43), channel_id=1, replica_groups=mesh['groups'=2,'seq'=4,'chan'=2,'rep'=2] {'chan','rep'}, use_global_device_ids=true, to_apply=%region_15.16 | all-reduce | flops 256 | bytes 2048 | tf_op jit(solution)/shard_map/psum | solution.py:260
  411.1 3.8 fusion.73
  414.9 38.6 %all-reduce.2.cloned.1.call-done = f32[256,512]{1,0:T(8,128)} async-done(((f32[256,512]{1,0:T(8,128)}), f32[256,512]{1,0:T(8,128)}) %all-reduce.2.cloned.1.call-update) | async-done | bytes 524304 | tf_op jit(solution)/shard_map/psum | solution.py:265
  453.5 1.3 exponential_reduce_fusion
  454.9 11.7 %psum.23 = f32[8]{0:T(128)S(1)} all-reduce(f32[8]{0:T(128)S(1)} %select_reduce_fusion.1), channel_id=1, replica_groups=mesh['groups'=2,'seq'=4,'chan'=2,'rep'=2] {'seq'}, use_global_device_ids=true, to_apply=%region_20.21 | all-reduce | flops 8 | bytes 64 | tf_op jit(solution)/shard_map/psum | solution.py:276
  (152 shorter events, 11.7 us)
Async XLA Ops:
  7.2 403.9 %copy-start = (bf16[2048,512]{1,0:T(8,128)(2,1)S(1)}, bf16[2048,512]{1,0:T(8,128)(2,1)}, u32[]{:S(2)}) copy-start(bf16[2048,512]{1,0:T(8,128)(2,1)} %param.27) | copy-start | bytes 6291460
  7.2 13.0 %copy-start.1 = (bf16[128,128]{1,0:T(8,128)(2,1)S(1)}, bf16[128,128]{1,0:T(8,128)(2,1)}, u32[]{:S(2)}) copy-start(bf16[128,128]{1,0:T(8,128)(2,1)} %param.23) | copy-start | bytes 98308
  7.2 446.3 %all-reduce.2.cloned.1.call-start = ((), (), s32[]{:S(2)}) async-start(), calls=%async_computation | async-start | bytes 1048576 | tf_op jit(solution)/shard_map/psum | solution.py:265
  8.8 248.4 %collective-permute-start = (bf16[2,8,2048]{2,1,0:T(8,128)(2,1)}, bf16[2,8,2048]{2,1,0:T(8,128)(2,1)}, u32[]{:S(2)}, u32[]{:S(2)}) collective-permute-start(bf16[2,8,2048]{2,1,0:T(8,128)(2,1)} %pad_maximum_fusion.1), channel_id=1, source_target_pairs={{0,4},{4,8},{8,12},{1,5},{5,9},{9,13},{2,6},{6,10},{10,14},{3,7},{... | collective-permute-start | bytes 196616 | tf_op jit(solution)/shard_map/ppermute | solution.py:16
  19.4 128.2 %copy-start.28 = (s32[2,128]{1,0:T(2,128)}, s32[2,128]{1,0:T(2,128)S(1)}, u32[]{:S(2)}) copy-start(s32[2,128]{1,0:T(2,128)S(1)} %get-tuple-element.844) | copy-start | bytes 3076
  134.3 12.9 %copy-start.13 = (f32[4,128,16]{1,2,0:T(8,128)S(1)}, f32[4,128,16]{1,2,0:T(8,128)}, u32[]{:S(2)}) copy-start(f32[4,128,16]{1,2,0:T(8,128)} %param.24) | copy-start | bytes 98308
  242.7 2.4 copy-start.2
  258.0 2.0 copy-start.8
  258.0 2.1 copy-start.9
  258.0 2.1 copy-start.10
  258.0 2.1 copy-start.11
  258.0 2.1 copy-start.12
  258.0 2.1 copy-start.18
  258.0 2.1 copy-start.19
  258.0 2.1 copy-start.20
  258.0 2.1 copy-start.21
  258.0 2.1 copy-start.22
  258.1 2.1 copy-start.23
  260.0 6.3 %slice-start = ((s8[8388608]{0:T(1024)(128)(4,1)}), s8[4194304]{0:T(1024)(128)(4,1)S(1)}, s32[]{:S(2)}) async-start(s8[8388608]{0:T(1024)(128)(4,1)} %bitcast.208), calls=%async_computation.1 | async-start | bytes 8388608
  260.1 6.2 %slice-start.1 = ((s8[8388608]{0:T(1024)(128)(4,1)}), s8[4194304]{0:T(1024)(128)(4,1)S(1)}, s32[]{:S(2)}) async-start(s8[8388608]{0:T(1024)(128)(4,1)} %bitcast.208), calls=%async_computation.2 | async-start | bytes 8388608
  263.2 13.8 %collective-permute-start.1 = (bf16[128,2048]{1,0:T(8,128)(2,1)S(1)}, bf16[128,2048]{1,0:T(8,128)(2,1)S(1)}, u32[]{:S(2)}, u32[]{:S(2)}) collective-permute-start(bf16[128,2048]{1,0:T(8,128)(2,1)S(1)} %slice.177), channel_id=1, source_target_pairs={{0,4},{4,8},{8,12},{1,5},{5,9},{9,13},{2,6},{6,10},{10,14},{3,7},{... | collective-permute-start | bytes 1572872 | tf_op jit(solution)/shard_map/ppermute | solution.py:16
  278.2 2.6 copy-start.14
  278.2 2.6 copy-start.24
  280.9 15.2 %copy-start.16 = (pred[2,128]{1,0:T(4,128)(4,1)S(1)}, pred[2,128]{1,0:T(4,128)(4,1)}, u32[]{:S(2)}) copy-start(pred[2,128]{1,0:T(4,128)(4,1)} %get-tuple-element.468) | copy-start | bytes 772
  296.1 2.4 copy-start.3
  296.1 2.4 copy-start.4
  300.5 3.5 copy-start.15
  300.5 3.5 copy-start.32
  376.2 4.8 %copy-start.29 = (s32[2,128]{1,0:T(2,128)S(1)}, s32[2,128]{1,0:T(2,128)}, u32[]{:S(2)}) copy-start(s32[2,128]{1,0:T(2,128)} %copy-done.28) | copy-start | bytes 3076
  381.0 16.2 %copy-start.17 = (f32[2,128]{1,0:T(2,128)S(1)}, f32[2,128]{1,0:T(2,128)}, u32[]{:S(2)}) copy-start(f32[2,128]{1,0:T(2,128)} %get-tuple-element.467) | copy-start | bytes 3076
  381.1 4.6 copy-start.6
  389.3 4.6 copy-start.6
  402.6 2.4 copy-start.7
  403.7 1.3 copy-start.5
  403.7 7.3 %copy-start.30 = (f32[2048]{0:T(1024)S(1)}, f32[2048]{0:T(1024)}, u32[]{:S(2)}) copy-start(f32[2048]{0:T(1024)} %param.26) | copy-start | bytes 24580
  411.1 42.5 %copy-start.27 = (s32[256]{0:T(256)S(1)}, s32[256]{0:T(256)}, u32[]{:S(2)}) copy-start(s32[256]{0:T(256)} %param.28) | copy-start | bytes 3076
  411.1 43.7 %copy-start.25 = (s32[256]{0:T(256)S(1)}, s32[256]{0:T(256)}, u32[]{:S(2)}) copy-start(s32[256]{0:T(256)} %get-tuple-element.821) | copy-start | bytes 3076
  411.1 55.5 %copy-start.31 = (s32[8]{0:T(128)S(1)}, s32[8]{0:T(128)}, u32[]{:S(2)}) copy-start(s32[8]{0:T(128)} %param.29) | copy-start | bytes 100
  454.8 12.3 %copy-start.26 = (f32[256]{0:T(256)}, f32[256]{0:T(256)S(1)}, u32[]{:S(2)}) copy-start(f32[256]{0:T(256)S(1)} %log_subtract_fusion) | copy-start | bytes 3076
Sparse Core Ops, SparseCore 0:
  415.1 38.4 all-reduce.1
where the time goes:
time: 476 us; the launch traced here: 474 us
  local copies, waits for them, and re-layouts  229 us (48%)
  blocking collectives  76.8 us (16%)
  other arithmetic  55.6 us (12%)
  waiting for transfers between devices  45.9 us (10%)
  matrix products  41.7 us (9%)
  between operations  14.6 us (3%)
  starting transfers between devices  8.67 us (2%)
    gather x2, local copies, waits for them, and re-layouts, medium_toeplitz(): jnp.take(medium_taps, jnp.clip(lag_grid, 0, tap_count - 1), axis=0)  127 us
    gather x2, local copies, waits for them, and re-layouts, modal_tables(): taken = jnp.take(kernel, jnp.clip(lag_grid, 0, tile_rows - 1), axis=0)  63.8 us
    all_gather x4, blocking collectives, entering_2(): gathered = jax.tree.map(lambda a: lax.all_gather(a, axis), part)  59.4 us
    psum x1, waiting for transfers between devices, per_device(): logits = lax.psum(partial_value, ('chan', 'rep'))  38.6 us
    dot_general x2, matrix products, medium_block(): jnp.einsum('gts,gis->git', matrix, window, preferred_element_type=jnp.flo...  12.2 us
    psum x1, blocking collectives, per_device(): totals = lax.psum(genome_part, 'seq')  11.7 us
  transfers between devices with their start and end apart: 3, of which 2 were waited for; matrix products, arithmetic and copies ran while one was open for 52% of the time, Pallas kernels for 0%

commit v1 on v0

--- a/solution.py
+++ b/solution.py
@@ -262,7 +262,7 @@
         jnp.bfloat16
     )
     partial_value = channel_logits(normed, unembed)
-    logits = lax.psum(partial_value, ("chan", "rep"))
+    logits = lax.psum(lax.psum(partial_value, "rep"), "chan")
     logprob = log_probs(logits, token_ids)
     genome_index = jnp.arange(genome_lengths.shape[0], dtype=jnp.int32)
     genome_part = jnp.sum(

time: 476 us -> 493 us (1.036)
  waiting for transfers between devices: 45.9 us -> 63.6 us
    psum x1 -> x2, waiting for transfers between devices: 38.6 us -> 56.3 us  [per_device(): logits = lax.psum(lax.psum(partial_value, 'rep'), 'chan')]
  transfers between devices with their start and end apart: 3 -> 4, of which waited for: 2 -> 3; matrix products, arithmetic and copies ran while one was open for 52% -> 50% of each run, Pallas kernels for 0% -> 0%
where the time goes in v1:
time: 493 us; the launch traced here: 492 us
  local copies, waits for them, and re-layouts  229 us (46%)
  blocking collectives  76.8 us (16%)
  waiting for transfers between devices  63.6 us (13%)
  other arithmetic  55.6 us (11%)
  matrix products  41.7 us (8%)
  between operations  14.6 us (3%)
  starting transfers between devices  8.71 us (2%)
    gather x2, local copies, waits for them, and re-layouts, medium_toeplitz(): jnp.take(medium_taps, jnp.clip(lag_grid, 0, tap_count - 1), axis=0)  127 us
    gather x2, local copies, waits for them, and re-layouts, modal_tables(): taken = jnp.take(kernel, jnp.clip(lag_grid, 0, tile_rows - 1), axis=0)  63.8 us
    all_gather x4, blocking collectives, entering_2(): gathered = jax.tree.map(lambda a: lax.all_gather(a, axis), part)  59.4 us
    psum x2, waiting for transfers between devices, per_device(): logits = lax.psum(lax.psum(partial_value, 'rep'), 'chan')  56.3 us
    dot_general x2, matrix products, medium_block(): jnp.einsum('gts,gis->git', matrix, window, preferred_element_type=jnp.flo...  12.2 us
    psum x1, blocking collectives, per_device(): totals = lax.psum(genome_part, 'seq')  11.7 us
  transfers between devices with their start and end apart: 4, of which 3 were waited for; matrix products, arithmetic and copies ran while one was open for 50% of the time, Pallas kernels for 0%

profile of v1, /device:TPU:0, one launch (start us, length us, event | category | flops | bytes accessed | tf_op | source)
XLA Modules:
  0.0 491.8 jit_solution(15063124474667674553)
XLA Ops:
  7.2 0.9 slice_bitcast_fusion.2
  8.8 5.5 %collective-permute-start = (bf16[2,8,2048]{2,1,0:T(8,128)(2,1)}, bf16[2,8,2048]{2,1,0:T(8,128)(2,1)}, u32[]{:S(2)}, u32[]{:S(2)}) collective-permute-start(bf16[2,8,2048]{2,1,0:T(8,128)(2,1)} %pad_maximum_fusion.1), channel_id=1, source_target_pairs={{0,4},{4,8},{8,12},{1,5},{5,9},{9,13},{2,6},{6,10},{10,14},{3,7},{... | collective-permute-start | bytes 196616 | tf_op jit(solution)/shard_map/ppermute | solution.py:16
  14.8 0.8 reduce-window.9
  16.3 0.7 compare_convert_fusion.8
  17.0 1.7 slice_convert_fusion.6
  20.1 114.1 %gather_fusion = bf16[32768,128]{1,0:T(8,128)(2,1)} fusion(bf16[128,128]{1,0:T(8,128)(2,1)S(1)} %copy-done.1, s32[32768]{0:T(1024)S(1)} %broadcast_clamp_fusion), kind=kCustom, calls=%fused_computation | custom fusion | bytes 16908288 | tf_op jit(solution)/shard_map/jit(_take)/gather | solution.py:62
  134.3 12.9 %copy.87 = bf16[128,256,128]{1,0,2:T(8,128)(2,1)} copy(bf16[128,256,128]{2,1,0:T(8,128)(2,1)} %bitcast.210) | data formatting | bytes 16777216 | tf_op jit(solution)/shard_map/jit(_take)/gather | solution.py:62
  147.9 9.5 %fusion.47 = (f32[129,128,16]{0,2,1:T(8,128)}, f32[129,128,16]{0,2,1:T(8,128)S(1)}, f32[129,128,16]{0,2,1:T(8,128)}) fusion(f32[128,16]{1,0:T(8,128)S(1)} %copy.90, f32[129]{0:T(256)S(1)} %iota_convert_fusion, f32[128,16]{1,0:T(8,128)S(1)} %copy.89, f32[129]{0:T(256)S(1)} %fusion.95, f32[128,16]{1,0:T(8,128)S(1)} %copy.91, f32[128,16]{1,0:T(8,128)S(1)} %copy.88), kind=kLoop, calls=%fused_computation.66 | loop fusion | flops 1849344 | bytes 3204104 | tf_op jit(solution)/shard_map/mul | solution.py:75
  157.4 1.4 fusion.101
  158.9 54.5 %gather_fusion.1 = f32[16384,128]{1,0:T(8,128)} fusion(f32[128,128]{1,0:T(8,128)S(1)} %copy.92, s32[16384]{0:T(1024)S(1)} %fusion.89), kind=kCustom, calls=%fused_computation.1 | custom fusion | bytes 16842752 | tf_op jit(solution)/shard_map/jit(_take)/gather | solution.py:83
  213.4 9.3 %copy.93 = f32[128,128,128]{1,0,2:T(8,128)} copy(f32[128,128,128]{2,1,0:T(8,128)} %bitcast.211) | data formatting | bytes 16777216 | tf_op jit(solution)/shard_map/jit(_take)/gather | solution.py:83
  222.7 4.5 fusion.76
  227.9 7.5 %select_bitcast_fusion = bf16[128,128,256]{2,1,0:T(8,128)(2,1)} fusion(bf16[128,256,128]{1,0,2:T(8,128)(2,1)} %copy.87, pred[128,256]{1,0:T(8,128)(4,1)S(1)} %get-tuple-element.472, pred[128,256]{1,0:T(8,128)(4,1)S(1)} %get-tuple-element.471), kind=kLoop, calls=%fused_computation.56 | loop fusion | flops 8388608 | bytes 16842752 | tf_op jit(solution)/shard_map/jit(_where)/select_n | solution.py:63
  235.4 6.8 %fusion.42 = bf16[128,128,128]{2,1,0:T(8,128)(2,1)} fusion(f32[128,128,128]{1,0,2:T(8,128)} %copy.93, pred[128,128]{1,0:T(8,128)(4,1)S(1)} %get-tuple-element.476, pred[128,128]{1,0:T(8,128)(4,1)S(1)} %get-tuple-element.475), kind=kLoop, calls=%fused_computation.54 | loop fusion | flops 12582912 | bytes 12615680 | tf_op jit(solution)/shard_map/convert_element_type | solution.py:97
  242.7 2.4 slice.179
  245.1 1.1 slice.180
  246.2 2.3 rev.6
  248.5 2.3 rev.7
  250.8 1.6 copy.94
  252.4 1.6 copy.95
  254.1 0.8 mul.500
  254.9 2.3 copy.85
  257.2 0.8 slice_bitcast_fusion
  258.1 1.9 convert_multiply_fusion.2
  260.1 3.0 fusion.51
  263.2 3.1 collective-permute-start.1
  266.3 3.4 bitcast_convert_fusion
  269.7 7.3 %collective-permute-done.1 = bf16[128,2048]{1,0:T(8,128)(2,1)S(1)} collective-permute-done((bf16[128,2048]{1,0:T(8,128)(2,1)S(1)}, bf16[128,2048]{1,0:T(8,128)(2,1)S(1)}, u32[]{:S(2)}, u32[]{:S(2)}) %collective-permute-start.1) | collective-permute-done | bytes 524320 | tf_op jit(solution)/shard_map/ppermute | solution.py:16
  277.0 1.3 maximum_bitcast_fusion.5
  278.2 2.6 copy.86
  280.9 15.2 %while.64 = (s32[]{:T(128)}, bf16[2,128,16,128]{3,2,1,0:T(8,128)(2,1)S(1)}, s32[2]{0:T(128)S(1)}, bf16[128,16,384]{2,1,0:T(8,128)(2,1)}, s32[256]{0:T(256)S(1)},...) while((s32[]{:T(128)}, bf16[2,128,16,128]{3,2,1,0:T(8,128)(2,1)S(1)}, ...), condition=%wide.region_5.6_spmd.clone, body=%wide.region_4.5_spmd.sunk.clone | while | flops 138706944 | bytes 10032308 | solution.py:184
  282.4 6.1 %fusion.126 = bf16[2,128,16,128]{3,2,1,0:T(8,128)(2,1)S(1)} fusion(bf16[2,128,16,128]{3,2,1,0:T(8,128)(2,1)S(1)} %get-tuple-element.826, s32[]{:T(128)} %get-tuple-element.825, bf16[128,128,256]{2,1,0:T(8,128)(2,1)} %get-tuple-element.839, pred[128,256]{1,0:T(8,128)(4,1)S(1)} %broadcast_compare_fusion.7, ...), kind=kOutput, calls=%fused_computation.8.clone.1.clone | convolution fusion | flops 138674176 | bytes 9994756 | tf_op jit(solution)/shard_map/while/body/eval_jaxpr/gts,gis->git/dot_general | solution.py:180
  290.0 6.1 %fusion.126 = bf16[2,128,16,128]{3,2,1,0:T(8,128)(2,1)S(1)} fusion(bf16[2,128,16,128]{3,2,1,0:T(8,128)(2,1)S(1)} %get-tuple-element.826, s32[]{:T(128)} %get-tuple-element.825, bf16[128,128,256]{2,1,0:T(8,128)(2,1)} %get-tuple-element.839, pred[128,256]{1,0:T(8,128)(4,1)S(1)} %broadcast_compare_fusion.7, ...), kind=kOutput, calls=%fused_computation.8.clone.1.clone | convolution fusion | flops 138674176 | bytes 9994756 | tf_op jit(solution)/shard_map/while/body/eval_jaxpr/gts,gis->git/dot_general | solution.py:180
  296.1 2.4 fusion.69
  298.5 2.0 add_bitcast_fusion
  300.5 3.5 copy.98
  304.0 7.3 %while.67 = (s32[]{:T(128)}, f32[128,16]{0,1:T(8,128)S(1)}, f32[128,16]{0,1:T(8,128)S(1)}, f32[128,16,16]{0,2,1:T(8,128)S(1)}, f32[128,16,16]{0,2,1:T(8,128)S(1)...) while((s32[]{:T(128)}, f32[128,16]{0,1:T(8,128)S(1)}, ...), condition=%wide.region_11.12_spmd.clone.clone, body=%wide.region_10.11_spmd.clone.sunk.clone | while | flops 421891 | bytes 2000031 | solution.py:229
  305.3 0.7 bitcast_dynamic-update-slice_fusion.9
  306.0 1.0 dynamic-slice_bitcast_fusion.3
  308.9 0.7 bitcast_dynamic-update-slice_fusion.9
  309.6 1.0 dynamic-slice_bitcast_fusion.3
  311.3 17.7 %all-gather.2 = f32[512,16,16]{0,2,1:T(8,128)} all-gather(f32[128,16,16]{0,2,1:T(8,128)S(1)} %get-tuple-element.221), channel_id=4, replica_groups=mesh['groups'=2,'seq'=4,'chan'=2,'rep'=2] {'seq'}, dimensions={0}, use_global_device_ids=true | all-gather | bytes 655360 | tf_op jit(solution)/shard_map/all_gather | solution.py:21
  329.0 2.1 reshape.364
  331.1 15.5 %all-gather.3 = f32[512,16,16]{0,2,1:T(8,128)} all-gather(f32[128,16,16]{0,2,1:T(8,128)S(1)} %get-tuple-element.222), channel_id=5, replica_groups=mesh['groups'=2,'seq'=4,'chan'=2,'rep'=2] {'seq'}, dimensions={0}, use_global_device_ids=true | all-gather | bytes 655360 | tf_op jit(solution)/shard_map/all_gather | solution.py:21
  346.5 2.0 reshape.365
  348.6 13.1 %all-gather = f32[512,16]{0,1:T(8,128)S(1)} all-gather(f32[128,16]{0,1:T(8,128)S(1)} %get-tuple-element.219), channel_id=2, replica_groups=mesh['groups'=2,'seq'=4,'chan'=2,'rep'=2] {'seq'}, dimensions={0}, use_global_device_ids=true | all-gather | bytes 40960 | tf_op jit(solution)/shard_map/all_gather | solution.py:21
  361.7 13.1 %all-gather.1 = f32[512,16]{0,1:T(8,128)S(1)} all-gather(f32[128,16]{0,1:T(8,128)S(1)} %get-tuple-element.220), channel_id=3, replica_groups=mesh['groups'=2,'seq'=4,'chan'=2,'rep'=2] {'seq'}, dimensions={0}, use_global_device_ids=true | all-gather | bytes 40960 | tf_op jit(solution)/shard_map/all_gather | solution.py:21
  375.1 1.1 multiply_subtract_fusion.2
  376.2 0.9 pad_maximum_fusion
  377.2 3.9 copy.103
  381.0 16.2 %while.65 = (s32[]{:T(128)}, f32[2,128,16,128]{3,2,0,1:T(8,128)}, bf16[2,128,16,128]{3,2,1,0:T(8,128)(2,1)S(1)}, s32[2,128]{1,0:T(2,128)S(1)}, bf16[128,128,128]{2,1,0:T(8,128)(2,1)}, /*index=5*/bf16[128,128,128]{2,1,0:T(8,128)(2,1)}) while((s32[]{:T(128)}, f32[2,128,16,128]{3,2,0,1:T(8,128)}, ...), condition=%wide.region_8.9_spmd.clone, body=%wide.region_7.8_spmd.sunk.clone | while | flops 138690560 | bytes 29411944 | solution.py:202
  381.2 4.6 fusion.132
  385.8 3.4 fusion.133
  389.3 4.6 fusion.132
  393.9 3.4 fusion.133
  397.3 5.3 %fusion.66 = f32[128,16,2,128]{3,1,2,0:T(8,128)S(1)} fusion(f32[2,128,16,128]{3,2,0,1:T(8,128)} %get-tuple-element.216, f32[2,128,16,32]{3,2,0,1:T(8,128)} %copy.103, f32[128,128,16]{0,2,1:T(8,128)} %get-tuple-element.440, f32[128,128,16]{0,2,1:T(8,128)} %get-tuple-element.438, bf16[2,128,16,128]{3,2,1,0:T(8,128)(2,1)S(1)} %get-tuple-element.924, ...), kind=kOutput, calls=%fused_computation.96 | convolution fusion | flops 204472320 | bytes 7873536 | tf_op jit(solution)/shard_map/gtm,jgim->jgit/dot_general | solution.py:244
  402.6 1.1 copy.106
  403.7 1.3 copy-done.5
  405.4 5.7 %psum.28 = f32[256]{0:T(256)S(1)} all-reduce(f32[256]{0:T(256)S(1)} %fusion.43), channel_id=1, replica_groups=mesh['groups'=2,'seq'=4,'chan'=2,'rep'=2] {'chan','rep'}, use_global_device_ids=true, to_apply=%region_15.16 | all-reduce | flops 256 | bytes 2048 | tf_op jit(solution)/shard_map/psum | solution.py:260
  411.1 3.8 fusion.73
  415.0 24.1 %all-reduce.3.cloned.1.call-done = f32[256,512]{1,0:T(8,128)} async-done(((f32[256,512]{1,0:T(8,128)}), f32[256,512]{1,0:T(8,128)}) %all-reduce.3.cloned.1.call-update) | async-done | bytes 524304 | tf_op jit(solution)/shard_map/psum | solution.py:265
  439.1 32.2 %all-reduce.5.cloned.1.call-done = f32[256,512]{1,0:T(8,128)} async-done(((f32[256,512]{1,0:T(8,128)}), f32[256,512]{1,0:T(8,128)}) %all-reduce.5.cloned.1.call-update) | async-done | bytes 524304 | tf_op jit(solution)/shard_map/psum | solution.py:265
  471.3 1.3 exponential_reduce_fusion
  472.7 11.7 %psum.31 = f32[8]{0:T(128)S(1)} all-reduce(f32[8]{0:T(128)S(1)} %select_reduce_fusion.1), channel_id=1, replica_groups=mesh['groups'=2,'seq'=4,'chan'=2,'rep'=2] {'seq'}, use_global_device_ids=true, to_apply=%region_21.22 | all-reduce | flops 8 | bytes 64 | tf_op jit(solution)/shard_map/psum | solution.py:276
  (155 shorter events, 12.5 us)
Async XLA Ops:
  7.2 403.9 %copy-start = (bf16[2048,512]{1,0:T(8,128)(2,1)S(1)}, bf16[2048,512]{1,0:T(8,128)(2,1)}, u32[]{:S(2)}) copy-start(bf16[2048,512]{1,0:T(8,128)(2,1)} %param.27) | copy-start | bytes 6291460
  7.2 13.0 %copy-start.1 = (bf16[128,128]{1,0:T(8,128)(2,1)S(1)}, bf16[128,128]{1,0:T(8,128)(2,1)}, u32[]{:S(2)}) copy-start(bf16[128,128]{1,0:T(8,128)(2,1)} %param.23) | copy-start | bytes 98308
  7.2 431.9 %all-reduce.3.cloned.1.call-start = ((), (), s32[]{:S(2)}) async-start(), calls=%async_computation | async-start | bytes 1048576 | tf_op jit(solution)/shard_map/psum | solution.py:265
  8.8 248.4 %collective-permute-start = (bf16[2,8,2048]{2,1,0:T(8,128)(2,1)}, bf16[2,8,2048]{2,1,0:T(8,128)(2,1)}, u32[]{:S(2)}, u32[]{:S(2)}) collective-permute-start(bf16[2,8,2048]{2,1,0:T(8,128)(2,1)} %pad_maximum_fusion.1), channel_id=1, source_target_pairs={{0,4},{4,8},{8,12},{1,5},{5,9},{9,13},{2,6},{6,10},{10,14},{3,7},{... | collective-permute-start | bytes 196616 | tf_op jit(solution)/shard_map/ppermute | solution.py:16
  19.4 128.2 %copy-start.28 = (s32[2,128]{1,0:T(2,128)}, s32[2,128]{1,0:T(2,128)S(1)}, u32[]{:S(2)}) copy-start(s32[2,128]{1,0:T(2,128)S(1)} %get-tuple-element.844) | copy-start | bytes 3076
  134.3 12.9 %copy-start.13 = (f32[4,128,16]{1,2,0:T(8,128)S(1)}, f32[4,128,16]{1,2,0:T(8,128)}, u32[]{:S(2)}) copy-start(f32[4,128,16]{1,2,0:T(8,128)} %param.24) | copy-start | bytes 98308
  242.7 2.4 copy-start.2
  258.0 2.0 copy-start.8
  258.0 2.1 copy-start.9
  258.0 2.1 copy-start.10
  258.0 2.1 copy-start.11
  258.0 2.1 copy-start.12
  258.0 2.1 copy-start.18
  258.0 2.1 copy-start.19
  258.0 2.1 copy-start.20
  258.0 2.1 copy-start.21
  258.0 2.1 copy-start.22
  258.1 2.1 copy-start.23
  260.0 6.3 %slice-start = ((s8[8388608]{0:T(1024)(128)(4,1)}), s8[4194304]{0:T(1024)(128)(4,1)S(1)}, s32[]{:S(2)}) async-start(s8[8388608]{0:T(1024)(128)(4,1)} %bitcast.208), calls=%async_computation.2 | async-start | bytes 8388608
  260.1 6.2 %slice-start.1 = ((s8[8388608]{0:T(1024)(128)(4,1)}), s8[4194304]{0:T(1024)(128)(4,1)S(1)}, s32[]{:S(2)}) async-start(s8[8388608]{0:T(1024)(128)(4,1)} %bitcast.208), calls=%async_computation.3 | async-start | bytes 8388608
  263.2 13.8 %collective-permute-start.1 = (bf16[128,2048]{1,0:T(8,128)(2,1)S(1)}, bf16[128,2048]{1,0:T(8,128)(2,1)S(1)}, u32[]{:S(2)}, u32[]{:S(2)}) collective-permute-start(bf16[128,2048]{1,0:T(8,128)(2,1)S(1)} %slice.177), channel_id=1, source_target_pairs={{0,4},{4,8},{8,12},{1,5},{5,9},{9,13},{2,6},{6,10},{10,14},{3,7},{... | collective-permute-start | bytes 1572872 | tf_op jit(solution)/shard_map/ppermute | solution.py:16
  278.2 2.6 copy-start.14
  278.2 2.6 copy-start.24
  280.9 15.2 %copy-start.16 = (pred[2,128]{1,0:T(4,128)(4,1)S(1)}, pred[2,128]{1,0:T(4,128)(4,1)}, u32[]{:S(2)}) copy-start(pred[2,128]{1,0:T(4,128)(4,1)} %get-tuple-element.468) | copy-start | bytes 772
  296.1 2.4 copy-start.3
  296.1 2.4 copy-start.4
  300.5 3.5 copy-start.15
  300.5 3.5 copy-start.32
  376.2 4.8 copy-start.29
  381.0 16.2 %copy-start.17 = (f32[2,128]{1,0:T(2,128)S(1)}, f32[2,128]{1,0:T(2,128)}, u32[]{:S(2)}) copy-start(f32[2,128]{1,0:T(2,128)} %get-tuple-element.467) | copy-start | bytes 3076
  381.1 4.6 copy-start.6
  389.3 4.6 copy-start.6
  402.6 2.4 copy-start.7
  403.7 1.3 copy-start.5
  403.7 7.3 %copy-start.30 = (f32[2048]{0:T(1024)S(1)}, f32[2048]{0:T(1024)}, u32[]{:S(2)}) copy-start(f32[2048]{0:T(1024)} %param.26) | copy-start | bytes 24580
  411.1 60.2 %copy-start.27 = (s32[256]{0:T(256)S(1)}, s32[256]{0:T(256)}, u32[]{:S(2)}) copy-start(s32[256]{0:T(256)} %param.28) | copy-start | bytes 3076
  411.1 61.5 %copy-start.25 = (s32[256]{0:T(256)S(1)}, s32[256]{0:T(256)}, u32[]{:S(2)}) copy-start(s32[256]{0:T(256)} %get-tuple-element.821) | copy-start | bytes 3076
  411.1 73.3 %copy-start.31 = (s32[8]{0:T(128)S(1)}, s32[8]{0:T(128)}, u32[]{:S(2)}) copy-start(s32[8]{0:T(128)} %param.29) | copy-start | bytes 100
  414.9 56.3 %all-reduce.5.cloned.1.call-start = ((), (), s32[]{:S(2)}) async-start(), calls=%async_computation.1 | async-start | bytes 1048576 | tf_op jit(solution)/shard_map/psum | solution.py:265
  472.6 12.3 %copy-start.26 = (f32[256]{0:T(256)}, f32[256]{0:T(256)S(1)}, u32[]{:S(2)}) copy-start(f32[256]{0:T(256)S(1)} %log_subtract_fusion) | copy-start | bytes 3076
Sparse Core Ops, SparseCore 0:
  415.1 23.9 all-reduce.2
  441.5 29.7 all-reduce.4
